TPU v7x, 32 devices: a whole 2x2x4 slice. The times are simulated.
32 devices in a mesh: sub: 2 (over core), row: 4 (over y, x), col: 4 (over z).
Axes of the slice: x: 2, y: 2, z: 4, core: 2. Of those that a mesh axis runs over, the one named last changes fastest.
Arguments:
- child: float32 [2, 6144, 6144], P('sub', 'row', 'col'), may hold values from -1 to 1
- row_map: int32 [2, 48], replicated, may hold values from 0 to 79, as said below
- col_map: int32 [2, 48], replicated, may hold values from 0 to 79, as said below
- own_diagonal: float32 [10240], P(('sub', 'col')), may hold values from 96 to 192
- coupling: float32 [10240, 512], P('row'), may hold values from -24 to 24
Outputs:
- factored: float32 [10240, 10240], P('row', ('sub', 'col'))
Inputs may be any that keep to these rules, and one draw needn't show every extreme that they name: For each child s the entries row_map[s, :] are distinct front blocks, always including block 0 and block 79, and they rise strictly along k = (p % 12) * 4 + p // 12. col_map[s, :] holds the same set of front blocks as row_map[s, :]; they rise strictly along k = (q % 12) * 4 + (q // 12 + 1) % 4.
All inputs are finite; a program needn't handle non-finite values.
Results may differ from a plain program's by a relative error of at most 0.00005.
Values sent between devices are 32-bit elements; how exact they have to be, the bound alone decides.
No kernel may reach another device: no remote copies, remote signals or barrier semaphores. Data moves between devices by JAX's collectives and lax.ppermute only.
A program may use at most 320 MiB of HBM per device.

v0:
```python
import jax
import jax.numpy as jnp
from jax import lax
from jax.sharding import PartitionSpec as P

FRONT = 10240
PANEL = 512
BLOCK = 128


def from_root(value, axis, source):
    kept = jnp.where(lax.axis_index(axis) == source, value, 0).astype(value.dtype)
    return lax.psum(kept, axis)


def block_routes(parent_blocks, per_source, per_target):
    number = parent_blocks.shape[0]
    positions = jnp.arange(number, dtype=jnp.int32)
    source = positions // per_source
    target = parent_blocks // per_target
    earlier = (
        (source[:, None] == source[None, :])
        & (target[:, None] == target[None, :])
        & (positions[None, :] < positions[:, None])
    )
    slot_index = jnp.sum(earlier.astype(jnp.int32), axis=1)
    return (positions, source, target, slot_index, parent_blocks % per_target)


def sending_table(parent_blocks, own_index, per_source, per_target, targets, capacity):
    positions, source, target, slot_index, local_block = block_routes(
        parent_blocks, per_source, per_target
    )
    wanted = jnp.arange(targets * capacity, dtype=jnp.int32)
    matches = (source == own_index)[None, :] & (
        (target * capacity + slot_index)[None, :] == wanted[:, None]
    )
    within = positions % per_source
    return jnp.where(
        jnp.any(matches, axis=1),
        jnp.sum(jnp.where(matches, within[None, :], 0), axis=1),
        per_source,
    )


def receiving_table(parent_blocks, own_index, per_source, per_target, capacity, offset, empty_slot):
    positions, source, target, slot_index, local_block = block_routes(
        parent_blocks, per_source, per_target
    )
    wanted = jnp.arange(per_target, dtype=jnp.int32)
    matches = (target == own_index)[None, :] & (local_block[None, :] == wanted[:, None])
    flat_slot = (source + offset) * capacity + slot_index
    return jnp.where(
        jnp.any(matches, axis=1),
        jnp.sum(jnp.where(matches, flat_slot[None, :], 0), axis=1),
        empty_slot,
    )


def with_zero(blocks, axis):
    shape = list(blocks.shape)
    shape[axis] = 1
    return jnp.concatenate([blocks, jnp.zeros(shape, blocks.dtype)], axis=axis)


def symmetric_of(corner):
    return jnp.tril(corner) + jnp.tril(corner, -1).T


def factor_corner(corner):
    lower = jnp.linalg.cholesky(symmetric_of(corner))
    inverse = jax.scipy.linalg.solve_triangular(
        lower, jnp.eye(PANEL, dtype=jnp.float32), lower=True
    )
    return (lower, inverse)


def apply_inverse(rows, inverse):
    return lax.dot_general(rows, inverse, (((1,), (1,)), ((), ())), precision=lax.Precision.HIGHEST)


def early_corner(child_piece, row_map, col_map, full_diagonal):
    n_row = lax.axis_size("row")
    n_col = lax.axis_size("col")
    n_sub = lax.axis_size("sub")
    rows_here, cols_here = child_piece.shape
    row_blocks = rows_here // BLOCK
    col_blocks = cols_here // BLOCK
    panel_blocks = PANEL // BLOCK
    first_rows = min(row_blocks, -(-panel_blocks // n_row))
    first_cols = min(col_blocks, -(-panel_blocks // n_col))
    piece = child_piece[: first_rows * BLOCK, : first_cols * BLOCK]
    pieces = lax.all_gather(piece, ("sub", "row", "col"))
    pieces = pieces.reshape(n_sub, n_row, n_col, first_rows, BLOCK, first_cols, BLOCK)
    pieces = pieces.transpose(0, 1, 3, 2, 5, 4, 6).reshape(
        n_sub, n_row * first_rows, n_col * first_cols, BLOCK, BLOCK
    )
    row_pos = (
        jnp.arange(n_row, dtype=jnp.int32)[:, None] * row_blocks
        + jnp.arange(first_rows, dtype=jnp.int32)[None, :]
    ).reshape(-1)
    col_pos = (
        jnp.arange(n_col, dtype=jnp.int32)[:, None] * col_blocks
        + jnp.arange(first_cols, dtype=jnp.int32)[None, :]
    ).reshape(-1)
    corner = jnp.zeros((panel_blocks + 1, panel_blocks + 1, BLOCK, BLOCK), jnp.float32)
    for which in range(n_sub):
        rb = row_map[which][row_pos]
        cb = col_map[which][col_pos]
        rb = jnp.where(rb < panel_blocks, rb, panel_blocks)
        cb = jnp.where(cb < panel_blocks, cb, panel_blocks)
        corner = corner.at[rb[:, None], cb[None, :]].add(pieces[which])
    corner = corner[:panel_blocks, :panel_blocks].transpose(0, 2, 1, 3).reshape(PANEL, PANEL)
    return corner + jnp.diag(full_diagonal[:PANEL])


def shards(child, row_map, col_map, own_diagonal, coupling):
    n_row = lax.axis_size("row")
    n_col = lax.axis_size("col")
    n_group = lax.axis_size(("sub", "col"))
    my_row = lax.axis_index("row")
    my_col = lax.axis_index("col")
    my_sub = lax.axis_index("sub")
    my_group = lax.axis_index(("sub", "col"))
    child_piece = child[0]
    rows_here, cols_here = child_piece.shape
    front_rows = FRONT // n_row
    front_cols = FRONT // n_group
    row_blocks = rows_here // BLOCK
    col_blocks = cols_here // BLOCK
    front_row_blocks = front_rows // BLOCK
    front_col_blocks = front_cols // BLOCK
    row_cap = min(row_blocks, (front_row_blocks + n_row - 1) // n_row)
    col_cap = min(col_blocks, (front_col_blocks + n_col - 1) // n_col)
    n_sub = lax.axis_size("sub")
    my_rows_map = lax.dynamic_index_in_dim(row_map, my_sub, 0, keepdims=False)
    my_cols_map = lax.dynamic_index_in_dim(col_map, my_sub, 0, keepdims=False)
    full_diagonal = from_root(own_diagonal[:PANEL], ("sub", "col"), 0)
    corner = early_corner(child_piece, row_map, col_map, full_diagonal)
    global_row = my_row * front_rows + jnp.arange(front_rows, dtype=jnp.int32)
    panel_blocks = PANEL // BLOCK
    first_cols = min(col_blocks, -(-panel_blocks // n_col))
    own_cands = child_piece[:, : first_cols * BLOCK].reshape(row_blocks, BLOCK, first_cols * BLOCK)
    pick_rows = sending_table(my_rows_map, my_row, row_blocks, front_row_blocks, n_row, row_cap)
    pick_rows = jnp.minimum(pick_rows, row_blocks - 1).reshape(n_row, row_cap)
    cand_send = own_cands.at[pick_rows].get(mode="promise_in_bounds")
    pieces = [lax.dynamic_index_in_dim(cand_send, my_row, 0, keepdims=False)]
    for shift in range(1, n_row):
        piece = lax.dynamic_index_in_dim(cand_send, (my_row + shift) % n_row, 0, keepdims=False)
        pieces.append(lax.ppermute(piece, "row", [(i, (i + shift) % n_row) for i in range(n_row)]))
    cand_got = jnp.stack(pieces).reshape(n_row * row_cap, BLOCK, first_cols * BLOCK)
    placement = receiving_table(
        my_rows_map, my_row, row_blocks, front_row_blocks, row_cap, 0, n_row * row_cap
    )
    row_valid = placement < n_row * row_cap
    source = jnp.minimum(placement, n_row * row_cap - 1) // row_cap
    placement = (my_row - source) % n_row * row_cap + placement % row_cap
    cand_rows = jnp.where(
        row_valid[:, None, None], cand_got.at[placement].get(mode="promise_in_bounds"), 0.0
    )
    cands = lax.all_gather(cand_rows, "col")
    cands = jnp.stack([cands, lax.ppermute(cands, "sub", [(0, 1), (1, 0)])])
    cands = cands.reshape(n_sub, n_col, front_row_blocks, BLOCK, first_cols, BLOCK)
    cands = cands.transpose(0, 1, 4, 2, 3, 5).reshape(
        n_sub, n_col * first_cols, front_row_blocks, BLOCK, BLOCK
    )
    cand_pos = (
        jnp.arange(n_col, dtype=jnp.int32)[:, None] * col_blocks
        + jnp.arange(first_cols, dtype=jnp.int32)[None, :]
    ).reshape(-1)
    panel_rows = None
    for which in range(n_sub):
        found = (
            col_map[which][cand_pos][None, :] == jnp.arange(panel_blocks, dtype=jnp.int32)[:, None]
        )
        pick = jnp.argmax(found, axis=1)
        mine = lax.dynamic_index_in_dim(cands, (which + my_sub) % n_sub, 0, keepdims=False)
        got = jnp.where(jnp.any(found, axis=1)[:, None, None, None], mine[pick], 0.0)
        panel_rows = got if panel_rows is None else panel_rows + got
    panel_rows = panel_rows.transpose(1, 2, 0, 3).reshape(front_rows, PANEL)
    panel_rows = panel_rows + jnp.where(global_row[:, None] >= PANEL, coupling, 0.0)
    panel_rows = panel_rows + jnp.where(
        global_row[:, None] == jnp.arange(PANEL, dtype=jnp.int32)[None, :],
        full_diagonal[None, :PANEL],
        0.0,
    )
    by_col = child_piece.reshape(rows_here, col_blocks, BLOCK)
    chosen = sending_table(my_cols_map, my_col, col_blocks, front_col_blocks, n_group, col_cap)
    chosen = jnp.minimum(chosen, col_blocks - 1).reshape(n_sub, n_col * col_cap)
    chosen = jnp.stack([chosen[1 - my_sub], chosen[my_sub]]).reshape(-1)
    outgoing = by_col.at[:, chosen].get(mode="promise_in_bounds")
    outgoing = outgoing.transpose(1, 0, 2).reshape(2, n_col, col_cap, rows_here, BLOCK)
    outgoing, corner = lax.optimization_barrier((outgoing, corner))
    lower, inverse = factor_corner(corner)
    other_half = lax.all_to_all(outgoing[0], "col", split_axis=0, concat_axis=0, tiled=True)
    other_half, lower, inverse, panel_rows = lax.optimization_barrier(
        (other_half, lower, inverse, panel_rows)
    )
    other_half = lax.ppermute(other_half, "sub", [(0, 1), (1, 0)])

    def row_sending(half, which):
        cols_of = lax.dynamic_index_in_dim(col_map, which, 0, keepdims=False)
        rows_of = lax.dynamic_index_in_dim(row_map, which, 0, keepdims=False)
        col_index = receiving_table(
            cols_of, my_group, col_blocks, front_col_blocks, col_cap, 0, n_col * col_cap
        )
        col_valid = col_index < n_col * col_cap
        col_index = jnp.minimum(col_index, n_col * col_cap - 1)
        row_index = sending_table(rows_of, my_row, row_blocks, front_row_blocks, n_row, row_cap)
        row_index = jnp.minimum(row_index, row_blocks - 1).reshape(n_row, row_cap)
        half = half.reshape(n_col * col_cap, row_blocks, BLOCK, BLOCK)
        sending = half.at[col_index[None, None, :], row_index[:, :, None]].get(
            mode="promise_in_bounds"
        )
        return (sending, col_valid, rows_of)

    def row_receiving(sending, col_valid, rows_of, by_permutes):
        placement = receiving_table(
            rows_of, my_row, row_blocks, front_row_blocks, row_cap, 0, n_row * row_cap
        )
        row_valid = placement < n_row * row_cap
        placement = jnp.minimum(placement, n_row * row_cap - 1)
        if by_permutes:
            pieces = [lax.dynamic_index_in_dim(sending, my_row, 0, keepdims=False)]
            for shift in range(1, n_row):
                piece = lax.dynamic_index_in_dim(
                    sending, (my_row + shift) % n_row, 0, keepdims=False
                )
                pairs = [(i, (i + shift) % n_row) for i in range(n_row)]
                pieces.append(lax.ppermute(piece, "row", pairs))
            received = jnp.stack(pieces)
            source = placement // row_cap
            placement = (my_row - source) % n_row * row_cap + placement % row_cap
        else:
            received = lax.all_to_all(sending, "row", split_axis=0, concat_axis=0, tiled=True)
        received = received.reshape(n_row * row_cap, front_col_blocks, BLOCK, BLOCK)
        part = received.at[placement].get(mode="promise_in_bounds")
        keep = row_valid[:, None] & col_valid[None, :]
        return (part, keep)

    sending_other, col_valid_other, rows_other = row_sending(other_half, 1 - my_sub)
    sending_other, own_outgoing = lax.optimization_barrier((sending_other, outgoing[1]))
    part_other, keep_other = row_receiving(sending_other, col_valid_other, rows_other, True)
    own_half = lax.all_to_all(own_outgoing, "col", split_axis=0, concat_axis=0, tiled=True)
    theirs_start = my_group * front_cols % front_rows
    theirs_root = my_group * front_cols // front_rows
    own_rows = apply_inverse(panel_rows, inverse)
    top_rows = jnp.where(my_row == 0, lower, own_rows[:PANEL])
    own_rows = jnp.concatenate([top_rows, own_rows[PANEL:]], axis=0)
    theirs = lax.dynamic_slice_in_dim(own_rows, theirs_start, front_cols, 0)
    theirs = from_root(theirs, "row", theirs_root)
    own_half, part_other, theirs = lax.optimization_barrier((own_half, part_other, theirs))
    sending_own, col_valid_own, rows_own = row_sending(own_half, my_sub)
    part_own, keep_own = row_receiving(sending_own, col_valid_own, rows_own, False)
    assembled = jnp.where(keep_other[:, :, None, None], part_other, 0.0) + jnp.where(
        keep_own[:, :, None, None], part_own, 0.0
    )
    assembled = assembled.transpose(0, 2, 1, 3).reshape(front_rows, front_cols)
    global_col = my_group * front_cols + jnp.arange(front_cols, dtype=jnp.int32)
    on_diagonal = global_row[:, None] == global_col[None, :]
    assembled = assembled + jnp.where(on_diagonal, own_diagonal[None, :], 0.0)
    coupling_wide = jnp.concatenate(
        [coupling, jnp.zeros((front_rows, front_cols - PANEL), jnp.float32)], axis=1
    )
    coupling_mask = (global_row[:, None] >= PANEL) & (global_col[None, :] < PANEL)
    front_part = assembled + jnp.where(coupling_mask, coupling_wide, 0.0)
    update = lax.dot_general(
        own_rows, theirs, (((1,), (1,)), ((), ())), precision=lax.Precision.HIGHEST
    )
    panel_wide = jnp.concatenate(
        [own_rows, jnp.zeros((front_rows, front_cols - PANEL), jnp.float32)], axis=1
    )
    trailing = front_part - update
    result = jnp.where(
        global_col[None, :] < PANEL,
        panel_wide,
        jnp.where(global_row[:, None] < PANEL, 0.0, trailing),
    )
    return result


def solution(mesh):
    placed = (P("sub", "row", "col"), P(), P(), P(("sub", "col")), P("row", None))
    return jax.shard_map(
        shards, mesh=mesh, in_specs=placed, out_specs=P("row", ("sub", "col")), check_vma=False
    )
```

profile of v0, /device:TPU:0, one launch (start us, length us, event | category | flops | bytes accessed | tf_op | source)
XLA Modules:
  0.0 902.3 jit_solution(14177149182014029454)
XLA Ops:
  12.7 3.0 collective-permute-start
  20.5 9.6 %copy.32 = f32[1,1536,1536]{1,2,0:T(8,128)} copy(f32[1,1536,1536]{2,1,0:T(8,128)} %param.5) | data formatting | bytes 18874368 | tf_op args[0]
  31.6 9.6 %copy.33 = f32[1536,12,128]{2,0,1:T(8,128)} copy(f32[1536,12,128]{0,2,1:T(8,128)} %bitcast.252) | data formatting | bytes 18874368 | tf_op jit(solution)/shard_map/reshape;squeeze | solution.py:187
  42.9 13.2 %gather_fusion = f32[24,1536,128]{2,1,0:T(8,128)} fusion(f32[1536,12,128]{2,0,1:T(8,128)} %copy.33, s32[1024]{0:T(1024)S(1)} %pad_clamp_fusion.7), kind=kCustom, calls=%fused_computation | custom fusion | bytes 37748832 | tf_op jit(solution)/shard_map/gather | solution.py:191
  56.8 15.9 %psum.14 = f32[512]{0:T(512)S(1)} all-reduce(f32[512]{0:T(512)S(1)} %slice_select_fusion.1), channel_id=1, replica_groups=mesh['sub'=2,'row'=4,'col'=4] {'sub','col'}, use_global_device_ids=true, to_apply=%region_5.6 | all-reduce | flops 512 | bytes 4096 | tf_op jit(solution)/shard_map/psum | solution.py:13
  76.8 2.6 fusion.98
  79.6 2.9 scatter_fusion
  85.2 14.0 %slice_bitcast_fusion = (f32[4,3,1536,128]{3,2,1,0:T(8,128)}, f32[4,3,1536,128]{3,2,1,0:T(8,128)}) fusion(f32[2,4,3,1536,128]{4,3,2,1,0:T(8,128)} %bitcast.248), kind=kLoop, calls=%fused_computation.28 | loop fusion | bytes 37748736 | tf_op jit(solution)/shard_map/squeeze | solution.py:242
  99.2 5.8 all-to-all-start
  110.7 11.7 %cholesky.103 = f32[128,128]{1,0:T(8,128)S(1)} custom-call(f32[128,128]{1,0:T(8,128)S(1)} %cholesky.263), custom_call_target="Cholesky" | custom-call | tf_op jit(solution)/shard_map/jit(cholesky)/cholesky | solution.py:71
  123.2 9.8 %custom-call.31 = f32[1,128,128]{1,2,0:T(8,128)S(1)} custom-call(f32[1,128,128]{2,1,0:T(8,128)S(1)} %get-tuple-element.94), custom_call_target="InvertDiagBlocksLowerTriangular" | custom-call | tf_op jit(solution)/shard_map/jit(cholesky)/cholesky | solution.py:71
  133.6 11.7 %cholesky.215 = f32[128,128]{1,0:T(8,128)S(1)} custom-call(f32[128,128]{1,0:T(8,128)S(1)} %cholesky.267), custom_call_target="Cholesky" | custom-call | tf_op jit(solution)/shard_map/jit(cholesky)/cholesky | solution.py:71
  146.0 9.9 %custom-call.32 = f32[1,128,128]{1,2,0:T(8,128)S(1)} custom-call(f32[1,128,128]{2,1,0:T(8,128)S(1)} %get-tuple-element.91), custom_call_target="InvertDiagBlocksLowerTriangular" | custom-call | tf_op jit(solution)/shard_map/jit(cholesky)/cholesky | solution.py:71
  155.9 103.4 %all-gather.4.cloned.1.call-done = f32[4,20,128,128]{3,2,1,0:T(8,128)} async-done(((f32[1,20,128,128]{3,2,1,0:T(8,128)}), f32[4,20,128,128]{3,2,1,0:T(8,128)}) %all-gather.4.cloned.1.call-update) | async-done | bytes 5242896 | tf_op jit(solution)/shard_map/all_gather | solution.py:161
  260.0 11.7 %cholesky.236 = f32[128,128]{1,0:T(8,128)S(1)} custom-call(f32[128,128]{1,0:T(8,128)S(1)} %cholesky.272), custom_call_target="Cholesky" | custom-call | tf_op jit(solution)/shard_map/jit(cholesky)/cholesky | solution.py:71
  271.8 9.8 %custom-call.33 = f32[1,128,128]{1,2,0:T(8,128)S(1)} custom-call(f32[1,128,128]{2,1,0:T(8,128)S(1)} %get-tuple-element.88), custom_call_target="InvertDiagBlocksLowerTriangular" | custom-call | tf_op jit(solution)/shard_map/jit(cholesky)/cholesky | solution.py:71
  282.2 11.9 %cholesky.253 = f32[128,128]{1,0:T(8,128)S(1)} custom-call(f32[128,128]{1,0:T(8,128)S(1)} %convolution_subtract_fusion.6), custom_call_target="Cholesky" | custom-call | tf_op jit(solution)/shard_map/jit(cholesky)/cholesky | solution.py:71
  302.6 10.8 %while.1 = (s32[]{:T(128)}, f32[512,512]{1,0:T(8,128)S(1)}, s32[4,2]{0,1:T(2,128)S(1)}, f32[4,128,128]{2,1,0:T(8,128)}, s32[]{:T(128)}) while((s32[]{:T(128)}, f32[512,512]{1,0:T(8,128)S(1)}, s32[4,2]{0,1:T(2,128)S(1)}, f32[4,128,128]{2,1,0:T(8,128)}, s32[]{:T(128)}) %tuple.85), condition=%wide.while_cond, body=%wide.while_body.sunk | while | flops 2 | bytes 132705 | solution.py:72
  303.3 2.0 bitcast_dynamic-update-slice_fusion.2
  306.0 2.0 bitcast_dynamic-update-slice_fusion.2
  308.6 2.0 bitcast_dynamic-update-slice_fusion.2
  311.3 2.0 bitcast_dynamic-update-slice_fusion.2
  313.4 40.1 %custom-call.34 = f32[4,128,128]{1,2,0:T(8,128)S(1)} custom-call(f32[4,128,128]{2,1,0:T(8,128)} %get-tuple-element.38), custom_call_target="InvertDiagBlocksLowerTriangular" | custom-call | tf_op jit(solution)/shard_map/jit(_solve_triangular)/triangular_solve | solution.py:72
  358.5 7.2 fusion.6
  365.8 5.8 gather_fusion.7
  371.5 5.7 gather_fusion.8
  377.3 5.4 add_bitcast_fusion.1
  382.7 3.9 copy.37
  386.7 4.0 fusion.7
  391.8 14.0 %collective-permute-done.4 = f32[4,3,1536,128]{3,2,1,0:T(8,128)} collective-permute-done((f32[4,3,1536,128]{3,2,1,0:T(8,128)}, f32[4,3,1536,128]{3,2,1,0:T(8,128)}, u32[]{:S(2)}, u32[]{:S(2)}) %collective-permute-start.4) | collective-permute-done | bytes 9437216 | tf_op jit(solution)/shard_map/ppermute | solution.py:199
  405.8 17.7 %gather_fusion.9 = f32[200,128,128]{2,1,0:T(8,128)} fusion(f32[12,12,128,128]{3,2,1,0:T(8,128)} %bitcast.65, s32[200]{0:T(256)S(1)} %reshape.928), kind=kCustom, calls=%fused_computation.9 | custom fusion | bytes 26216000 | tf_op jit(solution)/shard_map/gather | solution.py:212
  423.5 5.8 all-to-all-start.1
  429.5 9.1 %constant_dynamic-slice_fusion.1 = (f32[1,5,10,128,128]{4,3,2,1,0:T(8,128)S(1)}, f32[5,10,128,128]{3,2,1,0:T(8,128)}, f32[5,10,128,128]{3,2,1,0:T(8,128)}, f32[5,10,128,128]{3,2,1,0:T(8,128)}) fusion(f32[4,5,10,128,128]{4,3,2,1,0:T(8,128)} %bitcast.250, s32[]{:T(128)S(6)} %select_n.717, s32[]{:T(128)S(6)} %select_n.723, s32[]{:T(128)S(6)} %select_n.721, ...), kind=kLoop, calls=%fused_computation.165 | loop fusion | bytes 26214416 | tf_op jit(solution)/shard_map/jit(dynamic_index_in_dim)/dynamic_slice | solution.py:224
  443.0 10.7 %fusion.99 = f32[2560,512]{1,0:T(8,128)S(1)} fusion(f32[2560,512]{1,0:T(8,128)} %fusion.7, f32[512,512]{1,0:T(8,128)} %pad_maximum_fusion.3), kind=kOutput, calls=%fused_computation.328 | convolution fusion | flops 8053063680 | bytes 11534336 | tf_op jit(solution)/shard_map/dot_general | solution.py:79
  457.9 2.2 fusion.9
  460.6 67.1 %collective-permute-done.5 = f32[5,10,128,128]{3,2,1,0:T(8,128)} collective-permute-done((f32[5,10,128,128]{3,2,1,0:T(8,128)}, f32[5,10,128,128]{3,2,1,0:T(8,128)}, u32[]{:S(2)}, u32[]{:S(2)}) %collective-permute-start.5) | collective-permute-done | bytes 3276832 | tf_op jit(solution)/shard_map/ppermute | solution.py:230
  527.7 76.6 %collective-permute-done.6 = f32[5,10,128,128]{3,2,1,0:T(8,128)} collective-permute-done((f32[5,10,128,128]{3,2,1,0:T(8,128)}, f32[5,10,128,128]{3,2,1,0:T(8,128)}, u32[]{:S(2)}, u32[]{:S(2)}) %collective-permute-start.6) | collective-permute-done | bytes 3276832 | tf_op jit(solution)/shard_map/ppermute | solution.py:230
  604.3 9.0 pad_maximum_fusion
  613.3 12.6 %gather_fusion.10 = f32[20,10,128,128]{3,2,1,0:T(8,128)} fusion(f32[20,10,128,128]{3,2,1,0:T(8,128)} %bitcast.251, s32[1024]{0:T(1024)S(1)} %pad_clamp_fusion.1), kind=kCustom, calls=%fused_computation.10 | custom fusion | bytes 26214480 | tf_op jit(solution)/shard_map/gather | solution.py:237
  625.9 19.6 %all-reduce.5.cloned.1.call-done = f32[1280,512]{1,0:T(8,128)} async-done(((f32[1280,512]{1,0:T(8,128)}), f32[1280,512]{1,0:T(8,128)}) %all-reduce.5.cloned.1.call-update) | async-done | bytes 2621456 | tf_op jit(solution)/shard_map/psum | solution.py:13
  645.5 17.7 %gather_fusion.11 = f32[200,128,128]{2,1,0:T(8,128)} fusion(f32[12,12,128,128]{3,2,1,0:T(8,128)} %bitcast.83, s32[200]{0:T(256)S(1)} %reshape.942), kind=kCustom, calls=%fused_computation.11 | custom fusion | bytes 26216000 | tf_op jit(solution)/shard_map/gather | solution.py:212
  663.3 6.7 all-to-all-start.2
  670.3 5.0 pad_maximum_fusion.1
  675.3 137.9 %all-to-all-done.2 = f32[4,5,10,128,128]{4,3,2,1,0:T(8,128)} async-done(((f32[4,5,10,128,128]{4,3,2,1,0:T(8,128)}), f32[4,5,10,128,128]{4,3,2,1,0:T(8,128)}, u32[]{:S(2)}, u32[]{:S(2)}) %all-to-all-start.2) | async-done | bytes 13107232 | tf_op jit(solution)/shard_map/all_to_all | solution.py:235
  813.2 12.3 %gather_fusion.12 = f32[20,10,128,128]{3,2,1,0:T(8,128)} fusion(f32[20,10,128,128]{3,2,1,0:T(8,128)} %bitcast.85, s32[1024]{0:T(1024)S(1)} %pad_clamp_fusion), kind=kCustom, calls=%fused_computation.12 | custom fusion | bytes 26214480 | tf_op jit(solution)/shard_map/gather | solution.py:237
  825.5 9.3 %add_bitcast_fusion = f32[20,128,10,128]{3,1,2,0:T(8,128)S(1)} fusion(f32[20,10,128,128]{3,2,1,0:T(8,128)} %gather_fusion.12, f32[20,10,128,128]{3,2,1,0:T(8,128)} %gather_fusion.10, pred[20,10]{1,0:T(8,128)(4,1)S(1)} %broadcast_and_fusion, pred[20,10]{1,0:T(8,128)(4,1)S(1)} %broadcast_and_fusion.1), kind=kLoop, calls=%fused_computation.23 | loop fusion | flops 9830400 | bytes 39322000 | tf_op jit(solution)/shard_map/transpose | solution.py:258
  834.7 26.6 %copy.40 = f32[20,128,10,128]{3,2,1,0:T(8,128)S(1)} copy(f32[20,128,10,128]{3,1,2,0:T(8,128)S(1)} %add_bitcast_fusion) | data formatting | bytes 26214400 | tf_op jit(solution)/shard_map/reshape | solution.py:258
  861.3 34.2 %fusion.1 = f32[2560,1280]{1,0:T(8,128)} fusion(f32[2560,512]{1,0:T(8,128)} %pad_maximum_fusion.1, f32[1280,512]{1,0:T(8,128)} %all-reduce.5.cloned.1.call-done, f32[320,8,10,128]{3,2,1,0:T(8,128)S(1)} %bitcast.254, f32[2560,512]{1,0:T(8,128)} %param.9, f32[1280]{0:T(1024)S(1)} %copy-done.12, s32[1280]{0:T(1024)S(1)} %iota_add_fusion.1, ...), kind=kOutput, calls=%fused_computation.19 | convolution fusion | flops 20162150400 | bytes 39348480 | tf_op jit(solution)/shard_map/dot_general | solution.py:267
  (205 shorter events, 54.4 us)
Async XLA Ops:
  6.5 13.6 %copy-start.6 = (s32[2,48]{1,0:T(2,128)S(1)}, s32[2,48]{1,0:T(2,128)}, u32[]{:S(2)}) copy-start(s32[2,48]{1,0:T(2,128)} %param.7) | copy-start | bytes 1156
  6.5 70.2 %all-gather.6.cloned.1.call-start = ((), (), s32[]{:S(2)}) async-start(), calls=%async_computation.5 | async-start | bytes 2162688 | tf_op jit(solution)/shard_map/all_gather | solution.py:93
  12.7 60.3 %collective-permute-start = (f32[5,128,128]{2,1,0:T(8,128)S(1)}, f32[5,128,128]{2,1,0:T(8,128)S(1)}, u32[]{:S(2)}, u32[]{:S(2)}) collective-permute-start(f32[5,128,128]{2,1,0:T(8,128)S(1)} %get-tuple-element.83), channel_id=1, source_target_pairs={{0,4},{4,8},{8,12},{12,0},{1,5},{5,9},{9,13},{13,1},{2,6},{6,10},{... | collective-permute-start | bytes 983048 | tf_op jit(solution)/shard_map/ppermute | solution.py:150
  15.7 57.3 %collective-permute-start.1 = (f32[5,128,128]{2,1,0:T(8,128)S(1)}, f32[5,128,128]{2,1,0:T(8,128)S(1)}, u32[]{:S(2)}, u32[]{:S(2)}) collective-permute-start(f32[5,128,128]{2,1,0:T(8,128)S(1)} %get-tuple-element.82), channel_id=1, source_target_pairs={{0,8},{4,12},{8,0},{12,4},{1,9},{5,13},{9,1},{13,5},{2,10},{6,14},... | collective-permute-start | bytes 983048 | tf_op jit(solution)/shard_map/ppermute | solution.py:150
  17.2 55.8 %collective-permute-start.2 = (f32[5,128,128]{2,1,0:T(8,128)S(1)}, f32[5,128,128]{2,1,0:T(8,128)S(1)}, u32[]{:S(2)}, u32[]{:S(2)}) collective-permute-start(f32[5,128,128]{2,1,0:T(8,128)S(1)} %get-tuple-element.84), channel_id=1, source_target_pairs={{0,12},{4,0},{8,4},{12,8},{1,13},{5,1},{9,5},{13,9},{2,14},{6,2},{... | collective-permute-start | bytes 983048 | tf_op jit(solution)/shard_map/ppermute | solution.py:150
  20.1 239.2 %all-gather.4.cloned.1.call-start = ((), (), s32[]{:S(2)}) async-start(), calls=%async_computation.3 | async-start | bytes 6553600 | tf_op jit(solution)/shard_map/all_gather | solution.py:161
  31.6 9.6 %copy-start.7 = (s32[2,48]{1,0:T(2,128)S(1)}, s32[2,48]{1,0:T(2,128)}, u32[]{:S(2)}) copy-start(s32[2,48]{1,0:T(2,128)} %param.6) | copy-start | bytes 1156
  73.0 6.4 copy-start.8
  99.2 291.4 %all-to-all-start = ((f32[4,3,1536,128]{3,2,1,0:T(8,128)}), f32[4,3,1536,128]{3,2,1,0:T(8,128)}, u32[]{:S(2)}, u32[]{:S(2)}) async-start(f32[4,3,1536,128]{3,2,1,0:T(8,128)} %get-tuple-element.72), calls=%async_computation | async-start | bytes 18874368 | tf_op jit(solution)/shard_map/all_to_all | solution.py:195
  110.7 244.0 %copy-start.5 = (f32[512,512]{1,0:T(8,128)S(1)}, f32[512,512]{1,0:T(8,128)}, u32[]{:S(2)}) copy-start(f32[512,512]{1,0:T(8,128)} %fusion.18) | copy-start | bytes 3145732
  259.3 99.2 %collective-permute-start.3 = (f32[4,20,128,128]{3,2,1,0:T(8,128)}, f32[4,20,128,128]{3,2,1,0:T(8,128)}, u32[]{:S(2)}, u32[]{:S(2)}) collective-permute-start(f32[4,20,128,128]{3,2,1,0:T(8,128)} %all-gather.4.cloned.1.call-done), channel_id=1, source_target_pairs={{0,16},{16,0},{1,17},{17,1},{2,18},{18,2},{3,19},{19,3},{4,20},{20... | collective-permute-start | bytes 15728648 | tf_op jit(solution)/shard_map/ppermute | solution.py:162
  353.5 5.1 copy-start.3
  371.5 15.1 %slice-start = ((s8[5242880]{0:T(1024)(128)(4,1)}), s8[1048576]{0:T(1024)(128)(4,1)S(1)}, s32[]{:S(2)}) async-start(s8[5242880]{0:T(1024)(128)(4,1)} %bitcast.258), calls=%async_computation.6 | async-start | bytes 2097152
  377.3 9.3 %slice-start.1 = ((s8[5242880]{0:T(1024)(128)(4,1)}), s8[4194304]{0:T(1024)(128)(4,1)S(1)}, s32[]{:S(2)}) async-start(s8[5242880]{0:T(1024)(128)(4,1)} %bitcast.258), calls=%async_computation.7 | async-start | bytes 8388608
  386.6 4.6 copy-start.11
  386.6 4.6 copy-start.13
  386.7 4.8 copy-start.10
  390.7 15.1 %collective-permute-start.4 = (f32[4,3,1536,128]{3,2,1,0:T(8,128)}, f32[4,3,1536,128]{3,2,1,0:T(8,128)}, u32[]{:S(2)}, u32[]{:S(2)}) collective-permute-start(f32[4,3,1536,128]{3,2,1,0:T(8,128)} %all-to-all-done), channel_id=1, source_target_pairs={{0,16},{16,0},{1,17},{17,1},{2,18},{18,2},{3,19},{19,3},{4,20},{20... | collective-permute-start | bytes 28311560 | tf_op jit(solution)/shard_map/ppermute | solution.py:199
  423.5 222.0 %all-to-all-start.1 = ((f32[4,3,1536,128]{3,2,1,0:T(8,128)}), f32[4,3,1536,128]{3,2,1,0:T(8,128)}, u32[]{:S(2)}, u32[]{:S(2)}) async-start(f32[4,3,1536,128]{3,2,1,0:T(8,128)} %get-tuple-element.26), calls=%async_computation.1 | async-start | bytes 18874368 | tf_op jit(solution)/shard_map/all_to_all | solution.py:244
  429.3 216.2 %all-reduce.5.cloned.1.call-start = ((), (), s32[]{:S(2)}) async-start(), calls=%async_computation.4 | async-start | bytes 5242880 | tf_op jit(solution)/shard_map/psum | solution.py:13
  438.6 89.0 %collective-permute-start.5 = (f32[5,10,128,128]{3,2,1,0:T(8,128)}, f32[5,10,128,128]{3,2,1,0:T(8,128)}, u32[]{:S(2)}, u32[]{:S(2)}) collective-permute-start(f32[5,10,128,128]{3,2,1,0:T(8,128)} %get-tuple-element.76), channel_id=1, source_target_pairs={{0,4},{4,8},{8,12},{12,0},{1,5},{5,9},{9,13},{13,1},{2,6},{6,10},{... | collective-permute-start | bytes 9830408 | tf_op jit(solution)/shard_map/ppermute | solution.py:230
  440.0 164.3 %collective-permute-start.6 = (f32[5,10,128,128]{3,2,1,0:T(8,128)}, f32[5,10,128,128]{3,2,1,0:T(8,128)}, u32[]{:S(2)}, u32[]{:S(2)}) collective-permute-start(f32[5,10,128,128]{3,2,1,0:T(8,128)} %get-tuple-element.75), channel_id=1, source_target_pairs={{0,8},{4,12},{8,0},{12,4},{1,9},{5,13},{9,1},{13,5},{2,10},{6,14},... | collective-permute-start | bytes 9830408 | tf_op jit(solution)/shard_map/ppermute | solution.py:230
  441.8 162.5 %collective-permute-start.7 = (f32[5,10,128,128]{3,2,1,0:T(8,128)}, f32[5,10,128,128]{3,2,1,0:T(8,128)}, u32[]{:S(2)}, u32[]{:S(2)}) collective-permute-start(f32[5,10,128,128]{3,2,1,0:T(8,128)} %get-tuple-element.74), channel_id=1, source_target_pairs={{0,12},{4,0},{8,4},{12,8},{1,13},{5,1},{9,5},{13,9},{2,14},{6,2},{... | collective-permute-start | bytes 9830408 | tf_op jit(solution)/shard_map/ppermute | solution.py:230
  453.7 1.2 copy-start.4
  454.9 2.0 copy-start
  456.9 1.0 copy-start.1
  663.3 6.8 copy-start.9
  663.3 7.0 copy-start.2
  663.3 149.9 %all-to-all-start.2 = ((f32[4,5,10,128,128]{4,3,2,1,0:T(8,128)}), f32[4,5,10,128,128]{4,3,2,1,0:T(8,128)}, u32[]{:S(2)}, u32[]{:S(2)}) async-start(f32[4,5,10,128,128]{4,3,2,1,0:T(8,128)} %bitcast.249), calls=%async_computation.2 | async-start | bytes 26214400 | tf_op jit(solution)/shard_map/all_to_all | solution.py:235
  834.7 26.6 %copy-start.12 = (f32[1280]{0:T(1024)S(1)}, f32[1280]{0:T(1024)}, u32[]{:S(2)}) copy-start(f32[1280]{0:T(1024)} %param.8) | copy-start | bytes 15364
Sparse Core Ops, SparseCore 0:
  20.2 56.4 all-gather.5
  78.3 180.9 all-gather.3
  460.3 185.1 all-reduce.4
where the time goes:
time: 910 us; the launch traced here: 902 us
  waiting for transfers between devices  420 us (46%)
  local copies, waits for them, and re-layouts  185 us (20%)
  other arithmetic  184 us (20%)
  matrix products  50.7 us (6%)
  starting transfers between devices  29.4 us (3%)
  between operations  16.8 us (2%)
  blocking collectives  15.9 us (2%)
    ppermute x3, waiting for transfers between devices, row_receiving(): pieces.append(lax.ppermute(piece, 'row', pairs))  144 us
    all_to_all x1, waiting for transfers between devices, row_receiving(): lax.all_to_all(sending, 'row', split_axis=0, concat_axis=0, tiled=True)  138 us
    all_gather x1, waiting for transfers between devices, shards(): cands = lax.all_gather(cand_rows, 'col')  103 us
    another operation x15, other arithmetic, factor_corner(): lower = jnp.linalg.cholesky(symmetric_of(corner))  81.9 us
    another operation x4, other arithmetic, factor_corner(): jax.scipy.linalg.solve_triangular(lower, jnp.eye(PANEL, dtype=jnp.float32...  43 us
    gather x2, local copies, waits for them, and re-layouts, row_sending(): half.at[col_index[None, None, :], row_index[:, :, None]]  35.4 us
    dot_general x1, matrix products, shards(): lax.dot_general(own_rows, theirs, (((1,), (1,)), ((), ())), precision=lax...  34.2 us
    reshape x1, local copies, waits for them, and re-layouts, shards(): assembled = assembled.transpose(0, 2, 1, 3).reshape(front_rows, front_cols)  26.6 us
  transfers between devices with their start and end apart: 14, of which 7 were waited for; matrix products, arithmetic and copies ran while one was open for 32% of the time, Pallas kernels for 0%

commit v1 on v0

--- a/solution.py
+++ b/solution.py
@@ -10,7 +10,7 @@
 
 def from_root(value, axis, source):
     kept = jnp.where(lax.axis_index(axis) == source, value, 0).astype(value.dtype)
-    return lax.psum(kept, axis)
+    return jnp.sum(lax.all_gather(kept, axis), axis=0)
 
 
 def block_routes(parent_blocks, per_source, per_target):

time: 910 us -> 942 us (1.035)
  waiting for transfers between devices: 420 us -> 435 us
    ppermute x3, waiting for transfers between devices: 144 us -> 198 us  [row_receiving(): pieces.append(lax.ppermute(piece, 'row', pairs))]
    all_gather x0 -> x1, blocking collectives: none -> 21.8 us  [from_root(): return jnp.sum(lax.all_gather(kept, axis), axis=0)]
    psum x1 -> x0, waiting for transfers between devices: 19.6 us -> none  [from_root(): return lax.psum(kept, axis)]
    psum x1 -> x0, blocking collectives: 15.9 us -> none  [from_root(): return lax.psum(kept, axis)]
    ppermute x1, waiting for transfers between devices: 14 us -> 0.01 us  [shards(): other_half = lax.ppermute(other_half, 'sub', [(0, 1), (1, 0)])]
  transfers between devices with their start and end apart: 14 -> 14, of which waited for: 7 -> 4; matrix products, arithmetic and copies ran while one was open for 32% -> 35% of each run, Pallas kernels for 0% -> 0%
where the time goes in v1:
time: 942 us; the launch traced here: 934 us
  waiting for transfers between devices  435 us (46%)
  other arithmetic  190 us (20%)
  local copies, waits for them, and re-layouts  187 us (20%)
  matrix products  52.1 us (6%)
  starting transfers between devices  30.1 us (3%)
  blocking collectives  21.8 us (2%)
  between operations  17.1 us (2%)
    ppermute x3, waiting for transfers between devices, row_receiving(): pieces.append(lax.ppermute(piece, 'row', pairs))  198 us
    all_to_all x1, waiting for transfers between devices, row_receiving(): lax.all_to_all(sending, 'row', split_axis=0, concat_axis=0, tiled=True)  138 us
    all_gather x1, waiting for transfers between devices, shards(): cands = lax.all_gather(cand_rows, 'col')  98.6 us
    another operation x15, other arithmetic, factor_corner(): lower = jnp.linalg.cholesky(symmetric_of(corner))  81.9 us
    another operation x4, other arithmetic, factor_corner(): jax.scipy.linalg.solve_triangular(lower, jnp.eye(PANEL, dtype=jnp.float32...  42 us
    gather x2, local copies, waits for them, and re-layouts, row_sending(): half.at[col_index[None, None, :], row_index[:, :, None]]  35.4 us
    dot_general x1, matrix products, shards(): lax.dot_general(own_rows, theirs, (((1,), (1,)), ((), ())), precision=lax...  32.7 us
    reshape x1, local copies, waits for them, and re-layouts, shards(): assembled = assembled.transpose(0, 2, 1, 3).reshape(front_rows, front_cols)  26.6 us
  transfers between devices with their start and end apart: 14, of which 4 were waited for; matrix products, arithmetic and copies ran while one was open for 35% of the time, Pallas kernels for 0%

profile of v1, /device:TPU:0, one launch (start us, length us, event | category | flops | bytes accessed | tf_op | source)
XLA Modules:
  0.0 933.8 jit_solution(491633634133714658)
XLA Ops:
  12.6 3.0 collective-permute-start
  20.4 9.6 %copy.32 = f32[1,1536,1536]{1,2,0:T(8,128)} copy(f32[1,1536,1536]{2,1,0:T(8,128)} %param.5) | data formatting | bytes 18874368 | tf_op args[0]
  31.5 9.7 %copy.33 = f32[1536,12,128]{2,0,1:T(8,128)} copy(f32[1536,12,128]{0,2,1:T(8,128)} %bitcast.254) | data formatting | bytes 18874368 | tf_op jit(solution)/shard_map/reshape;squeeze | solution.py:187
  43.6 21.8 %all-gather.3 = f32[8,1,512]{2,1,0:T(1,128)S(1)} all-gather(f32[1,1,512]{2,1,0:T(1,128)S(1)} %bitcast.272), channel_id=3, replica_groups=mesh['sub'=2,'row'=4,'col'=4] {'sub','col'}, dimensions={0}, use_global_device_ids=true | all-gather | bytes 18432 | tf_op jit(solution)/shard_map/all_gather | solution.py:13
  65.5 13.4 %gather_fusion = f32[24,1536,128]{2,1,0:T(8,128)} fusion(f32[1536,12,128]{2,0,1:T(8,128)} %copy.33, s32[1024]{0:T(1024)S(1)} %pad_clamp_fusion.7), kind=kCustom, calls=%fused_computation | custom fusion | bytes 37748832 | tf_op jit(solution)/shard_map/gather | solution.py:191
  81.3 2.6 fusion.98
  84.1 3.0 scatter_fusion
  89.8 13.4 %slice_bitcast_fusion = (f32[4,3,1536,128]{3,2,1,0:T(8,128)}, f32[4,3,1536,128]{3,2,1,0:T(8,128)}) fusion(f32[2,4,3,1536,128]{4,3,2,1,0:T(8,128)} %bitcast.250), kind=kLoop, calls=%fused_computation.28 | loop fusion | bytes 37748736 | tf_op jit(solution)/shard_map/squeeze | solution.py:242
  103.2 5.8 all-to-all-start
  114.9 11.7 %cholesky.103 = f32[128,128]{1,0:T(8,128)S(1)} custom-call(f32[128,128]{1,0:T(8,128)S(1)} %cholesky.263), custom_call_target="Cholesky" | custom-call | tf_op jit(solution)/shard_map/jit(cholesky)/cholesky | solution.py:71
  127.4 9.8 %custom-call.31 = f32[1,128,128]{1,2,0:T(8,128)S(1)} custom-call(f32[1,128,128]{2,1,0:T(8,128)S(1)} %get-tuple-element.94), custom_call_target="InvertDiagBlocksLowerTriangular" | custom-call | tf_op jit(solution)/shard_map/jit(cholesky)/cholesky | solution.py:71
  137.9 11.7 %cholesky.215 = f32[128,128]{1,0:T(8,128)S(1)} custom-call(f32[128,128]{1,0:T(8,128)S(1)} %cholesky.267), custom_call_target="Cholesky" | custom-call | tf_op jit(solution)/shard_map/jit(cholesky)/cholesky | solution.py:71
  150.1 9.9 %custom-call.32 = f32[1,128,128]{1,2,0:T(8,128)S(1)} custom-call(f32[1,128,128]{2,1,0:T(8,128)S(1)} %get-tuple-element.91), custom_call_target="InvertDiagBlocksLowerTriangular" | custom-call | tf_op jit(solution)/shard_map/jit(cholesky)/cholesky | solution.py:71
  160.1 98.6 %all-gather.8.cloned.1.call-done = f32[4,20,128,128]{3,2,1,0:T(8,128)} async-done(((f32[1,20,128,128]{3,2,1,0:T(8,128)}), f32[4,20,128,128]{3,2,1,0:T(8,128)}) %all-gather.8.cloned.1.call-update) | async-done | bytes 5242896 | tf_op jit(solution)/shard_map/all_gather | solution.py:161
  259.3 11.7 %cholesky.236 = f32[128,128]{1,0:T(8,128)S(1)} custom-call(f32[128,128]{1,0:T(8,128)S(1)} %cholesky.272), custom_call_target="Cholesky" | custom-call | tf_op jit(solution)/shard_map/jit(cholesky)/cholesky | solution.py:71
  271.1 9.8 %custom-call.33 = f32[1,128,128]{1,2,0:T(8,128)S(1)} custom-call(f32[1,128,128]{2,1,0:T(8,128)S(1)} %get-tuple-element.88), custom_call_target="InvertDiagBlocksLowerTriangular" | custom-call | tf_op jit(solution)/shard_map/jit(cholesky)/cholesky | solution.py:71
  281.5 11.9 %cholesky.253 = f32[128,128]{1,0:T(8,128)S(1)} custom-call(f32[128,128]{1,0:T(8,128)S(1)} %convolution_subtract_fusion.6), custom_call_target="Cholesky" | custom-call | tf_op jit(solution)/shard_map/jit(cholesky)/cholesky | solution.py:71
  301.9 14.3 %while.1 = (s32[]{:T(128)}, f32[512,512]{1,0:T(8,128)}, s32[4,2]{0,1:T(2,128)S(1)}, f32[4,128,128]{2,1,0:T(8,128)}, s32[]{:T(128)}) while((s32[]{:T(128)}, f32[512,512]{1,0:T(8,128)}, s32[4,2]{0,1:T(2,128)S(1)}, f32[4,128,128]{2,1,0:T(8,128)}, s32[]{:T(128)}) %tuple.85), condition=%wide.while_cond, body=%wide.while_body.sunk | while | flops 2 | bytes 132705 | solution.py:72
  302.6 2.9 bitcast_dynamic-update-slice_fusion.2
  306.2 2.9 bitcast_dynamic-update-slice_fusion.2
  309.8 2.9 bitcast_dynamic-update-slice_fusion.2
  313.4 2.9 bitcast_dynamic-update-slice_fusion.2
  316.2 40.1 %custom-call.34 = f32[4,128,128]{1,2,0:T(8,128)S(1)} custom-call(f32[4,128,128]{2,1,0:T(8,128)} %get-tuple-element.38), custom_call_target="InvertDiagBlocksLowerTriangular" | custom-call | tf_op jit(solution)/shard_map/jit(_solve_triangular)/triangular_solve | solution.py:72
  363.5 7.3 fusion.6
  370.7 5.8 gather_fusion.7
  376.5 5.8 gather_fusion.8
  382.3 5.4 add_bitcast_fusion.1
  387.8 3.9 copy.37
  391.7 4.0 fusion.7
  396.1 10.6 %fusion.99 = f32[2560,512]{1,0:T(8,128)S(1)} fusion(f32[2560,512]{1,0:T(8,128)} %fusion.7, f32[512,512]{1,0:T(8,128)S(1)} %pad_maximum_fusion.3), kind=kOutput, calls=%fused_computation.328 | convolution fusion | flops 8053063680 | bytes 11534336 | tf_op jit(solution)/shard_map/dot_general | solution.py:79
  410.1 2.3 fusion.9
  413.1 17.7 %gather_fusion.9 = f32[200,128,128]{2,1,0:T(8,128)} fusion(f32[12,12,128,128]{3,2,1,0:T(8,128)} %bitcast.66, s32[200]{0:T(256)S(1)} %reshape.928), kind=kCustom, calls=%fused_computation.9 | custom fusion | bytes 26216000 | tf_op jit(solution)/shard_map/gather | solution.py:212
  430.8 5.8 all-to-all-start.1
  436.6 9.1 constant_dynamic-slice_fusion.1
  445.7 2.3 collective-permute-start.5
  451.3 72.6 %collective-permute-done.5 = f32[5,10,128,128]{3,2,1,0:T(8,128)} collective-permute-done((f32[5,10,128,128]{3,2,1,0:T(8,128)}, f32[5,10,128,128]{3,2,1,0:T(8,128)}, u32[]{:S(2)}, u32[]{:S(2)}) %collective-permute-start.5) | collective-permute-done | bytes 3276832 | tf_op jit(solution)/shard_map/ppermute | solution.py:230
  523.9 125.7 %collective-permute-done.6 = f32[5,10,128,128]{3,2,1,0:T(8,128)} collective-permute-done((f32[5,10,128,128]{3,2,1,0:T(8,128)}, f32[5,10,128,128]{3,2,1,0:T(8,128)}, u32[]{:S(2)}, u32[]{:S(2)}) %collective-permute-start.6) | collective-permute-done | bytes 3276832 | tf_op jit(solution)/shard_map/ppermute | solution.py:230
  649.7 9.2 pad_maximum_fusion
  658.8 12.4 %gather_fusion.10 = f32[20,10,128,128]{3,2,1,0:T(8,128)} fusion(f32[20,10,128,128]{3,2,1,0:T(8,128)} %bitcast.253, s32[1024]{0:T(1024)S(1)} %pad_clamp_fusion.1), kind=kCustom, calls=%fused_computation.10 | custom fusion | bytes 26214480 | tf_op jit(solution)/shard_map/gather | solution.py:237
  671.2 7.1 reduce_sum.165
  678.3 17.7 %gather_fusion.11 = f32[200,128,128]{2,1,0:T(8,128)} fusion(f32[12,12,128,128]{3,2,1,0:T(8,128)} %bitcast.85, s32[200]{0:T(256)S(1)} %reshape.942), kind=kCustom, calls=%fused_computation.11 | custom fusion | bytes 26216000 | tf_op jit(solution)/shard_map/gather | solution.py:212
  696.0 6.8 all-to-all-start.2
  703.0 5.2 pad_maximum_fusion.1
  708.2 137.8 %all-to-all-done.2 = f32[4,5,10,128,128]{4,3,2,1,0:T(8,128)} async-done(((f32[4,5,10,128,128]{4,3,2,1,0:T(8,128)}), f32[4,5,10,128,128]{4,3,2,1,0:T(8,128)}, u32[]{:S(2)}, u32[]{:S(2)}) %all-to-all-start.2) | async-done | bytes 13107232 | tf_op jit(solution)/shard_map/all_to_all | solution.py:235
  846.0 12.3 %gather_fusion.12 = f32[20,10,128,128]{3,2,1,0:T(8,128)} fusion(f32[20,10,128,128]{3,2,1,0:T(8,128)} %bitcast.87, s32[1024]{0:T(1024)S(1)} %pad_clamp_fusion), kind=kCustom, calls=%fused_computation.12 | custom fusion | bytes 26214480 | tf_op jit(solution)/shard_map/gather | solution.py:237
  858.3 9.3 add_bitcast_fusion
  867.5 26.6 %copy.40 = f32[20,128,10,128]{3,2,1,0:T(8,128)S(1)} copy(f32[20,128,10,128]{3,1,2,0:T(8,128)S(1)} %add_bitcast_fusion) | data formatting | bytes 26214400 | tf_op jit(solution)/shard_map/reshape | solution.py:258
  894.1 32.7 %fusion.1 = f32[2560,1280]{1,0:T(8,128)} fusion(f32[2560,512]{1,0:T(8,128)} %pad_maximum_fusion.1, f32[1280,512]{1,0:T(8,128)S(1)} %copy-done.5, f32[320,8,10,128]{3,2,1,0:T(8,128)S(1)} %bitcast.256, f32[2560,512]{1,0:T(8,128)} %param.9, f32[1280]{0:T(1024)S(1)} %copy-done.12, s32[1280]{0:T(1024)S(1)} %iota_add_fusion.1, s32[2560]{0:T(1024)S(1)} %iota_add_fusion, ...), kind=kOutput, calls=%fused_computation.19 | convolution fusion | flops 20162150400 | bytes 39348480 | tf_op jit(solution)/shard_map/dot_general | solution.py:267
  (207 shorter events, 52.3 us)
Async XLA Ops:
  6.5 13.6 %copy-start.6 = (s32[2,48]{1,0:T(2,128)S(1)}, s32[2,48]{1,0:T(2,128)}, u32[]{:S(2)}) copy-start(s32[2,48]{1,0:T(2,128)} %param.7) | copy-start | bytes 1156
  6.5 74.7 %all-gather.10.cloned.1.call-start = ((), (), s32[]{:S(2)}) async-start(), calls=%async_computation.4 | async-start | bytes 2162688 | tf_op jit(solution)/shard_map/all_gather | solution.py:93
  12.6 66.6 %collective-permute-start = (f32[5,128,128]{2,1,0:T(8,128)S(1)}, f32[5,128,128]{2,1,0:T(8,128)S(1)}, u32[]{:S(2)}, u32[]{:S(2)}) collective-permute-start(f32[5,128,128]{2,1,0:T(8,128)S(1)} %get-tuple-element.83), channel_id=1, source_target_pairs={{0,4},{4,8},{8,12},{12,0},{1,5},{5,9},{9,13},{13,1},{2,6},{6,10},{... | collective-permute-start | bytes 983048 | tf_op jit(solution)/shard_map/ppermute | solution.py:150
  15.6 63.6 %collective-permute-start.1 = (f32[5,128,128]{2,1,0:T(8,128)S(1)}, f32[5,128,128]{2,1,0:T(8,128)S(1)}, u32[]{:S(2)}, u32[]{:S(2)}) collective-permute-start(f32[5,128,128]{2,1,0:T(8,128)S(1)} %get-tuple-element.82), channel_id=1, source_target_pairs={{0,8},{4,12},{8,0},{12,4},{1,9},{5,13},{9,1},{13,5},{2,10},{6,14},... | collective-permute-start | bytes 983048 | tf_op jit(solution)/shard_map/ppermute | solution.py:150
  17.1 62.1 %collective-permute-start.2 = (f32[5,128,128]{2,1,0:T(8,128)S(1)}, f32[5,128,128]{2,1,0:T(8,128)S(1)}, u32[]{:S(2)}, u32[]{:S(2)}) collective-permute-start(f32[5,128,128]{2,1,0:T(8,128)S(1)} %get-tuple-element.84), channel_id=1, source_target_pairs={{0,12},{4,0},{8,4},{12,8},{1,13},{5,1},{9,5},{13,9},{2,14},{6,2},{... | collective-permute-start | bytes 983048 | tf_op jit(solution)/shard_map/ppermute | solution.py:150
  20.0 238.6 %all-gather.8.cloned.1.call-start = ((), (), s32[]{:S(2)}) async-start(), calls=%async_computation.3 | async-start | bytes 6553600 | tf_op jit(solution)/shard_map/all_gather | solution.py:161
  31.5 9.7 %copy-start.7 = (s32[2,48]{1,0:T(2,128)S(1)}, s32[2,48]{1,0:T(2,128)}, u32[]{:S(2)}) copy-start(s32[2,48]{1,0:T(2,128)} %param.6) | copy-start | bytes 1156
  79.2 4.7 copy-start.8
  103.2 292.4 %all-to-all-start = ((f32[4,3,1536,128]{3,2,1,0:T(8,128)}), f32[4,3,1536,128]{3,2,1,0:T(8,128)}, u32[]{:S(2)}, u32[]{:S(2)}) async-start(f32[4,3,1536,128]{3,2,1,0:T(8,128)} %get-tuple-element.72), calls=%async_computation | async-start | bytes 18874368 | tf_op jit(solution)/shard_map/all_to_all | solution.py:195
  109.0 562.2 %all-gather.12.cloned.1.call-start = ((), (), s32[]{:S(2)}) async-start(), calls=%async_computation.5 | async-start | bytes 13107200 | tf_op jit(solution)/shard_map/all_gather | solution.py:13
  114.9 242.7 %copy-start.4 = (f32[512,512]{1,0:T(8,128)S(1)}, f32[512,512]{1,0:T(8,128)}, u32[]{:S(2)}) copy-start(f32[512,512]{1,0:T(8,128)} %fusion.18) | copy-start | bytes 3145732
  258.6 104.8 %collective-permute-start.3 = (f32[4,20,128,128]{3,2,1,0:T(8,128)}, f32[4,20,128,128]{3,2,1,0:T(8,128)}, u32[]{:S(2)}, u32[]{:S(2)}) collective-permute-start(f32[4,20,128,128]{3,2,1,0:T(8,128)} %all-gather.8.cloned.1.call-done), channel_id=1, source_target_pairs={{0,16},{16,0},{1,17},{17,1},{2,18},{18,2},{3,19},{19,3},{4,20},{20... | collective-permute-start | bytes 15728648 | tf_op jit(solution)/shard_map/ppermute | solution.py:162
  356.4 7.1 copy-start.3
  376.5 15.2 %slice-start = ((s8[5242880]{0:T(1024)(128)(4,1)}), s8[1048576]{0:T(1024)(128)(4,1)S(1)}, s32[]{:S(2)}) async-start(s8[5242880]{0:T(1024)(128)(4,1)} %bitcast.261), calls=%async_computation.6 | async-start | bytes 2097152
  382.3 9.3 slice-start.1
  395.6 17.4 %collective-permute-start.4 = (f32[4,3,1536,128]{3,2,1,0:T(8,128)}, f32[4,3,1536,128]{3,2,1,0:T(8,128)}, u32[]{:S(2)}, u32[]{:S(2)}) collective-permute-start(f32[4,3,1536,128]{3,2,1,0:T(8,128)} %all-to-all-done), channel_id=1, source_target_pairs={{0,16},{16,0},{1,17},{17,1},{2,18},{18,2},{3,19},{19,3},{4,20},{20... | collective-permute-start | bytes 28311560 | tf_op jit(solution)/shard_map/ppermute | solution.py:199
  407.2 1.9 copy-start
  409.1 0.9 copy-start.1
  410.1 2.4 copy-start.11
  410.1 2.4 copy-start.13
  410.1 2.6 copy-start.10
  430.8 247.5 %all-to-all-start.1 = ((f32[4,3,1536,128]{3,2,1,0:T(8,128)}), f32[4,3,1536,128]{3,2,1,0:T(8,128)}, u32[]{:S(2)}, u32[]{:S(2)}) async-start(f32[4,3,1536,128]{3,2,1,0:T(8,128)} %get-tuple-element.26), calls=%async_computation.1 | async-start | bytes 18874368 | tf_op jit(solution)/shard_map/all_to_all | solution.py:244
  445.7 78.2 %collective-permute-start.5 = (f32[5,10,128,128]{3,2,1,0:T(8,128)}, f32[5,10,128,128]{3,2,1,0:T(8,128)}, u32[]{:S(2)}, u32[]{:S(2)}) collective-permute-start(f32[5,10,128,128]{3,2,1,0:T(8,128)} %get-tuple-element.76), channel_id=1, source_target_pairs={{0,4},{4,8},{8,12},{12,0},{1,5},{5,9},{9,13},{13,1},{2,6},{6,10},{... | collective-permute-start | bytes 9830408 | tf_op jit(solution)/shard_map/ppermute | solution.py:230
  448.0 201.7 %collective-permute-start.6 = (f32[5,10,128,128]{3,2,1,0:T(8,128)}, f32[5,10,128,128]{3,2,1,0:T(8,128)}, u32[]{:S(2)}, u32[]{:S(2)}) collective-permute-start(f32[5,10,128,128]{3,2,1,0:T(8,128)} %get-tuple-element.75), channel_id=1, source_target_pairs={{0,8},{4,12},{8,0},{12,4},{1,9},{5,13},{9,1},{13,5},{2,10},{6,14},... | collective-permute-start | bytes 9830408 | tf_op jit(solution)/shard_map/ppermute | solution.py:230
  450.0 199.7 %collective-permute-start.7 = (f32[5,10,128,128]{3,2,1,0:T(8,128)}, f32[5,10,128,128]{3,2,1,0:T(8,128)}, u32[]{:S(2)}, u32[]{:S(2)}) collective-permute-start(f32[5,10,128,128]{3,2,1,0:T(8,128)} %get-tuple-element.74), channel_id=1, source_target_pairs={{0,12},{4,0},{8,4},{12,8},{1,13},{5,1},{9,5},{13,9},{2,14},{6,2},{... | collective-permute-start | bytes 9830408 | tf_op jit(solution)/shard_map/ppermute | solution.py:230
  696.0 6.9 copy-start.9
  696.0 7.0 copy-start.2
  696.0 150.0 %all-to-all-start.2 = ((f32[4,5,10,128,128]{4,3,2,1,0:T(8,128)}), f32[4,5,10,128,128]{4,3,2,1,0:T(8,128)}, u32[]{:S(2)}, u32[]{:S(2)}) async-start(f32[4,5,10,128,128]{4,3,2,1,0:T(8,128)} %bitcast.251), calls=%async_computation.2 | async-start | bytes 26214400 | tf_op jit(solution)/shard_map/all_to_all | solution.py:235
  867.5 26.6 %copy-start.5 = (f32[1280,512]{1,0:T(8,128)S(1)}, f32[1280,512]{1,0:T(8,128)}, u32[]{:S(2)}) copy-start(f32[1280,512]{1,0:T(8,128)} %reduce_sum.165) | copy-start | bytes 7864324
  867.5 26.6 %copy-start.12 = (f32[1280]{0:T(1024)S(1)}, f32[1280]{0:T(1024)}, u32[]{:S(2)}) copy-start(f32[1280]{0:T(1024)} %param.8) | copy-start | bytes 15364
Sparse Core Ops, SparseCore 0:
  20.2 56.4 all-gather.9
  81.4 177.2 all-gather.7
  412.5 232.2 all-gather.11
